TPU v7x, 32 devices: a whole 2x2x4 slice. The times are simulated.
32 devices in a mesh: grp: 4 (over x, core), ep: 8 (over z, y).
Axes of the slice: x: 2, y: 2, z: 4, core: 2. Of those that a mesh axis runs over, the one named last changes fastest.
Arguments:
- tokens: bfloat16 [2048, 5120], P('ep', 'grp'), may hold values from -6 to 6
- cotangent: bfloat16 [2048, 5120], P('ep', 'grp'), may hold values from -0.59765625 to 0.59765625
- gate_weights: bfloat16 [2048, 6], P('ep'), may hold values from 0.099609375 to 1
- expert_ids: int32 [2048, 6], P('ep'), may hold values from 0 to 159, all different within a row; in each aligned block of 256 rows (0 to 255, 256 to 511, ...) at most 16 rows name the same one
- hot_ids: int32 [2], replicated, may hold values from 8 to 159, as said below
- gate_cold: bfloat16 [8, 5120, 768], P('ep', 'grp'), may hold values from -0.078125 to 0.078125
- up_cold: bfloat16 [8, 5120, 768], P('ep', 'grp'), may hold values from -0.078125 to 0.078125
- down_cold: bfloat16 [8, 768, 5120], P('ep', None, 'grp'), may hold values from -0.21875 to 0.21875
- gate_hot: bfloat16 [2, 5120, 768], P(None, 'grp', 'ep'), may hold values from -0.078125 to 0.078125
- up_hot: bfloat16 [2, 5120, 768], P(None, 'grp', 'ep'), may hold values from -0.078125 to 0.078125
- down_hot: bfloat16 [2, 768, 5120], P(None, 'ep', 'grp'), may hold values from -0.21875 to 0.21875
Outputs:
- grad_gate_cold: bfloat16 [8, 5120, 768], P('ep', 'grp')
- grad_up_cold: bfloat16 [8, 5120, 768], P('ep', 'grp')
- grad_down_cold: bfloat16 [8, 768, 5120], P('ep', None, 'grp')
- grad_gate_hot: float32 [2, 5120, 768], P(None, 'grp', 'ep')
- grad_up_hot: float32 [2, 5120, 768], P(None, 'grp', 'ep')
- grad_down_hot: float32 [2, 768, 5120], P(None, 'ep', 'grp')
- gate_weight_grad: float32 [2048, 6], P('ep')
Inputs may be any that keep to these rules, and one draw needn't show every extreme that they name: `expert_ids`: each row names 6 different experts. Among the routes of the 256 tokens of one index of ep (aligned blocks of rows) no expert is named more than 16 times, a bound that some block reaches. `hot_ids`: distinct expert numbers, none below 8; expert 160 - 1 is always among them.
All inputs are finite; a program needn't handle non-finite values.
Results may differ from a plain program's by a relative error of at most 0.02.
Values may be sent and summed in bfloat16 or wider, within the bound.
No kernel may reach another device: no remote copies, remote signals or barrier semaphores. Data moves between devices by JAX's collectives and lax.ppermute only.
A program may use at most 128 MiB of HBM per device.

v0:
```python
import jax
import jax.numpy as jnp
from jax import lax
from jax.sharding import PartitionSpec as P


def route_table(flat_ids, targets, capacity):
    matches = (flat_ids[:, None] == targets[None, :]).astype(jnp.int32)
    rank_of = jnp.cumsum(matches, axis=0) - 1
    slot_of = jnp.sum(matches * rank_of, axis=1)
    owner_of = jnp.sum(matches * jnp.arange(targets.shape[0], dtype=jnp.int32)[None, :], axis=1)
    usable = jnp.sum(matches, axis=1) > 0
    row_of = owner_of * capacity + slot_of
    rows_total = targets.shape[0] * capacity
    route_map = (row_of[None, :] == jnp.arange(rows_total, dtype=jnp.int32)[:, None]) & usable[
        None, :
    ]
    return route_map.astype(jnp.float32)


def gather_rows(route_map, tokens, cotangent, flat_weights, tok_rows, top_count):
    per_token = jnp.sum(route_map.reshape(route_map.shape[0], tok_rows, top_count), axis=2)
    token_map = per_token.astype(jnp.bfloat16)
    feat_rows = jnp.dot(token_map, tokens, preferred_element_type=jnp.float32).astype(jnp.bfloat16)
    cotan_rows = jnp.dot(token_map, cotangent, preferred_element_type=jnp.float32).astype(
        jnp.bfloat16
    )
    scale_rows = jnp.dot(
        route_map, flat_weights.astype(jnp.float32), precision=lax.Precision.HIGHEST
    )
    return (feat_rows, cotan_rows, scale_rows.astype(jnp.bfloat16))


def swiglu_back(pre_gate, pre_up, grad_hidden):
    sigmoid_gate = jax.nn.sigmoid(pre_gate)
    activated = pre_gate * sigmoid_gate
    hidden = (activated * pre_up).astype(jnp.bfloat16)
    back_gate = (
        grad_hidden * pre_up * sigmoid_gate * (1.0 + pre_gate * (1.0 - sigmoid_gate))
    ).astype(jnp.bfloat16)
    back_up = (grad_hidden * activated).astype(jnp.bfloat16)
    return (hidden, back_gate, back_up)


def body(
    tokens,
    cotangent,
    gate_weights,
    expert_ids,
    hot_ids,
    gate_cold,
    up_cold,
    down_cold,
    gate_hot,
    up_hot,
    down_hot,
):
    tok_rows, slice_width = tokens.shape
    top_count = expert_ids.shape[1]
    cold_count = lax.axis_size("ep")
    hot_count = hot_ids.shape[0]
    capacity = tok_rows // 16
    flat_ids = expert_ids.reshape(-1)
    flat_weights = gate_weights.reshape(-1)
    cold_map = route_table(flat_ids, jnp.arange(cold_count, dtype=jnp.int32), capacity)
    hot_map = route_table(flat_ids, hot_ids, capacity)
    cold_feats, cold_cotan, cold_scale = gather_rows(
        cold_map, tokens, cotangent, flat_weights, tok_rows, top_count
    )
    hot_feats, hot_cotan, hot_scale = gather_rows(
        hot_map, tokens, cotangent, flat_weights, tok_rows, top_count
    )
    outgoing = (
        cold_feats.reshape(cold_count, capacity, slice_width),
        cold_cotan.reshape(cold_count, capacity, slice_width),
        cold_scale.reshape(cold_count, capacity),
    )
    recv_feats, recv_cotan, recv_scale = (
        lax.all_to_all(outgoing[0], "ep", split_axis=0, concat_axis=0, tiled=True),
        lax.all_to_all(outgoing[1], "ep", split_axis=0, concat_axis=0, tiled=True),
        lax.all_to_all(outgoing[2], "ep", split_axis=0, concat_axis=0, tiled=True),
    )
    recv_feats = recv_feats.reshape(-1, slice_width)
    recv_cotan = recv_cotan.reshape(-1, slice_width)
    weighted = (
        recv_scale.reshape(-1).astype(jnp.float32)[:, None] * recv_cotan.astype(jnp.float32)
    ).astype(jnp.bfloat16)
    w_gate = gate_cold[0]
    w_up = up_cold[0]
    w_down = down_cold[0]
    part_gate = jnp.dot(recv_feats, w_gate, preferred_element_type=jnp.float32)
    part_up = jnp.dot(recv_feats, w_up, preferred_element_type=jnp.float32)
    part_hidden = lax.dot_general(
        weighted, w_down, (((1,), (1,)), ((), ())), preferred_element_type=jnp.float32
    )
    pre_gate, pre_up, grad_hidden = (
        lax.psum(part_gate.astype(jnp.bfloat16), "grp").astype(jnp.float32),
        lax.psum(part_up.astype(jnp.bfloat16), "grp").astype(jnp.float32),
        lax.psum(part_hidden.astype(jnp.bfloat16), "grp").astype(jnp.float32),
    )
    hidden, back_gate, back_up = swiglu_back(pre_gate, pre_up, grad_hidden)
    output_slice = jnp.dot(hidden, w_down, preferred_element_type=jnp.float32)
    cold_route = jnp.sum(output_slice * recv_cotan.astype(jnp.float32), axis=1)
    contract_rows = (((0,), (0,)), ((), ()))
    grad_gate_cold = lax.dot_general(
        recv_feats, back_gate, contract_rows, preferred_element_type=jnp.float32
    )
    grad_up_cold = lax.dot_general(
        recv_feats, back_up, contract_rows, preferred_element_type=jnp.float32
    )
    grad_down_cold = lax.dot_general(
        hidden, weighted, contract_rows, preferred_element_type=jnp.float32
    )
    hot_feats = hot_feats.reshape(hot_count, capacity, slice_width)
    hot_cotan = hot_cotan.reshape(hot_count, capacity, slice_width)
    hot_scale = hot_scale.reshape(hot_count, capacity)
    full_gate, full_up = (
        lax.all_gather(gate_hot, "ep", axis=2, tiled=True),
        lax.all_gather(up_hot, "ep", axis=2, tiled=True),
    )
    full_down = lax.all_gather(down_hot, "ep", axis=1, tiled=True)
    hot_weighted = (
        hot_scale.astype(jnp.float32)[:, :, None] * hot_cotan.astype(jnp.float32)
    ).astype(jnp.bfloat16)
    part_gate_hot = jnp.einsum(
        "jcd,jdh->jch", hot_feats, full_gate, preferred_element_type=jnp.float32
    )
    part_up_hot = jnp.einsum("jcd,jdh->jch", hot_feats, full_up, preferred_element_type=jnp.float32)
    part_hidden_hot = jnp.einsum(
        "jcd,jhd->jch", hot_weighted, full_down, preferred_element_type=jnp.float32
    )
    pre_gate_hot, pre_up_hot, grad_hidden_hot = (
        lax.psum(part_gate_hot.astype(jnp.bfloat16), "grp").astype(jnp.float32),
        lax.psum(part_up_hot.astype(jnp.bfloat16), "grp").astype(jnp.float32),
        lax.psum(part_hidden_hot.astype(jnp.bfloat16), "grp").astype(jnp.float32),
    )
    hidden_hot, back_gate_hot, back_up_hot = swiglu_back(pre_gate_hot, pre_up_hot, grad_hidden_hot)
    output_hot = jnp.einsum(
        "jch,jhd->jcd", hidden_hot, full_down, preferred_element_type=jnp.float32
    )
    hot_route_part = jnp.sum(output_hot * hot_cotan.astype(jnp.float32), axis=2)
    shadow_gate = jnp.einsum(
        "jcd,jch->jdh", hot_feats, back_gate_hot, preferred_element_type=jnp.float32
    )
    shadow_up = jnp.einsum(
        "jcd,jch->jdh", hot_feats, back_up_hot, preferred_element_type=jnp.float32
    )
    shadow_down = jnp.einsum(
        "jch,jcd->jdh", hidden_hot, hot_weighted, preferred_element_type=jnp.float32
    )
    grad_gate_hot, grad_up_hot, down_turned = (
        lax.psum_scatter(
            shadow_gate.astype(jnp.bfloat16), "ep", scatter_dimension=2, tiled=True
        ).astype(jnp.float32),
        lax.psum_scatter(
            shadow_up.astype(jnp.bfloat16), "ep", scatter_dimension=2, tiled=True
        ).astype(jnp.float32),
        lax.psum_scatter(
            shadow_down.astype(jnp.bfloat16), "ep", scatter_dimension=2, tiled=True
        ).astype(jnp.float32),
    )
    grad_down_hot = jnp.transpose(down_turned, (0, 2, 1))
    cold_route, hot_route = lax.psum((cold_route, hot_route_part), "grp")
    cold_back = lax.all_to_all(
        cold_route.reshape(cold_count, capacity), "ep", split_axis=0, concat_axis=0, tiled=True
    )
    route_flat = jnp.dot(cold_back.reshape(-1), cold_map, precision=lax.Precision.HIGHEST)
    route_flat = route_flat + jnp.dot(
        hot_route.reshape(-1), hot_map, precision=lax.Precision.HIGHEST
    )
    gate_weight_grad = route_flat.reshape(tok_rows, top_count)
    return (
        grad_gate_cold[None].astype(jnp.bfloat16),
        grad_up_cold[None].astype(jnp.bfloat16),
        grad_down_cold[None].astype(jnp.bfloat16),
        grad_gate_hot,
        grad_up_hot,
        grad_down_hot,
        gate_weight_grad,
    )


def solution(mesh):
    in_specs = (
        P("ep", "grp"),
        P("ep", "grp"),
        P("ep", None),
        P("ep", None),
        P(),
        P("ep", "grp", None),
        P("ep", "grp", None),
        P("ep", None, "grp"),
        P(None, "grp", "ep"),
        P(None, "grp", "ep"),
        P(None, "ep", "grp"),
    )
    out_specs = (
        P("ep", "grp", None),
        P("ep", "grp", None),
        P("ep", None, "grp"),
        P(None, "grp", "ep"),
        P(None, "grp", "ep"),
        P(None, "ep", "grp"),
        P("ep", None),
    )
    return jax.shard_map(body, mesh=mesh, in_specs=in_specs, out_specs=out_specs, check_vma=False)
```

profile of v0, /device:TPU:0, one launch (start us, length us, event | category | flops | bytes accessed | tf_op | source)
XLA Modules:
  0.0 574.7 jit_solution(6589414462695450256)
XLA Ops:
  8.0 0.7 all-gather.6.cloned.1.call-update
  9.4 1.5 copy.29
  10.9 1.0 eq.93
  12.0 1.0 eq.88
  13.0 0.8 copy.33
  14.0 2.3 reduce-window.14
  17.2 0.7 all_to_all.24
  17.9 7.3 %all-to-all-start.1 = ((bf16[8,1,16]{2,1,0:T(2,128)(2,1)}), bf16[8,1,16]{2,1,0:T(2,128)(2,1)S(1)}, u32[]{:S(2)}, u32[]{:S(2)}) async-start(bf16[8,1,16]{2,1,0:T(2,128)(2,1)} %all_to_all.24), calls=%async_computation.1 | async-start | bytes 8192 | tf_op jit(solution)/shard_map/all_to_all | solution.py:81
  25.2 0.8 add.66
  26.1 0.7 compare_convert_fusion.1
  27.9 0.8 fusion.77
  28.7 0.8 add.70
  29.5 1.0 copy.36
  30.7 1.0 copy.31
  32.3 1.0 convolution_convert_fusion.7
  33.5 6.0 %all-to-all-start = ((bf16[8,16,1280]{2,1,0:T(8,128)(2,1)}), bf16[8,16,1280]{2,1,0:T(8,128)(2,1)S(1)}, u32[]{:S(2)}, u32[]{:S(2)}) async-start(bf16[8,16,1280]{2,1,0:T(8,128)(2,1)} %bitcast.121), calls=%async_computation | async-start | bytes 655360 | tf_op jit(solution)/shard_map/all_to_all | solution.py:79
  39.8 1.0 convolution_convert_fusion.6
  40.7 11.0 %all-to-all-done = bf16[8,16,1280]{2,1,0:T(8,128)(2,1)S(1)} async-done(((bf16[8,16,1280]{2,1,0:T(8,128)(2,1)}), bf16[8,16,1280]{2,1,0:T(8,128)(2,1)S(1)}, u32[]{:S(2)}, u32[]{:S(2)}) %all-to-all-start) | async-done | bytes 327712 | tf_op jit(solution)/shard_map/all_to_all | solution.py:79
  51.8 5.0 all-to-all-start.2
  56.8 2.7 fusion.16
  59.4 2.7 fusion.19
  62.1 13.3 %all-to-all-done.2 = bf16[8,16,1280]{2,1,0:T(8,128)(2,1)S(1)} async-done(((bf16[8,16,1280]{2,1,0:T(8,128)(2,1)}), bf16[8,16,1280]{2,1,0:T(8,128)(2,1)S(1)}, u32[]{:S(2)}, u32[]{:S(2)}) %all-to-all-start.2) | async-done | bytes 327712 | tf_op jit(solution)/shard_map/all_to_all | solution.py:80
  75.5 12.9 %all-gather.8.cloned.1.call-done = bf16[2,1280,768]{1,2,0:T(8,128)(2,1)} async-done(((bf16[2,1280,96]{1,2,0:T(8,128)(2,1)}), bf16[2,1280,768]{1,2,0:T(8,128)(2,1)}) %all-gather.8.cloned.1.call-update) | async-done | bytes 3932176 | tf_op jit(solution)/shard_map/all_gather | solution.py:118
  88.4 3.9 convolution_convert_fusion.10
  92.3 67.5 %all-gather.6.cloned.1.call-done = bf16[2,1280,768]{1,2,0:T(8,128)(2,1)} async-done(((bf16[2,1280,96]{1,2,0:T(8,128)(2,1)}), bf16[2,1280,768]{1,2,0:T(8,128)(2,1)}) %all-gather.6.cloned.1.call-update) | async-done | bytes 3932176 | tf_op jit(solution)/shard_map/all_gather | solution.py:119
  159.7 3.9 convolution_convert_fusion.11
  163.6 66.8 %all-gather.4.cloned.1.call-done = bf16[2,768,1280]{2,1,0:T(8,128)(2,1)} async-done(((bf16[2,96,1280]{2,1,0:T(8,128)(2,1)}), bf16[2,768,1280]{2,1,0:T(8,128)(2,1)}) %all-gather.4.cloned.1.call-update) | async-done | bytes 3932176 | tf_op jit(solution)/shard_map/all_gather | solution.py:121
  230.4 3.9 convolution_convert_fusion.12
  234.4 1.5 fusion.13
  235.9 27.8 %all-reduce.6.cloned.1.call-done = (bf16[2,16,768]{2,1,0:T(8,128)(2,1)}, bf16[2,16,768]{2,1,0:T(8,128)(2,1)}, bf16[2,16,768]{2,1,0:T(8,128)(2,1)}) async-done(((bf16[2,16,768]{2,1,0:T(8,128)(2,1)}, bf16[2,16,768]{2,1,0:T(8,128)(2,1)}, bf16[2,16,768]{2,1,0:T(8,128)(2,1)}), (bf16[2,16,768]{2,1,0:T(8,128)(2,1)}, bf16[2,16,768]{2,1,0:T(8,128)(2,1)}, bf16[2,16,768]{2,1,0:T(8,128)(2,1)})) %all-reduce.6.cloned.1.call-update) | async-done | bytes 147472 | tf_op jit(solution)/shard_map/psum | solution.py:134
  263.8 4.0 convolution_convert_fusion.1
  267.9 3.2 convolution_convert_fusion
  271.4 3.2 convolution_convert_fusion.2
  274.8 26.7 %all-reduce.8.cloned.1.call-done = (bf16[128,768]{1,0:T(8,128)(2,1)}, bf16[128,768]{1,0:T(8,128)(2,1)}, bf16[128,768]{1,0:T(8,128)(2,1)}) async-done(((bf16[128,768]{1,0:T(8,128)(2,1)}, bf16[128,768]{1,0:T(8,128)(2,1)}, bf16[128,768]{1,0:T(8,128)(2,1)}), (bf16[128,768]{1,0:T(8,128)(2,1)}, bf16[128,768]{1,0:T(8,128)(2,1)}, bf16[128,768]{1,0:T(8,128)(2,1)})) %all-reduce.8.cloned.1.call-update) | async-done | bytes 589840 | tf_op jit(solution)/shard_map/psum | solution.py:98
  301.5 1.6 fusion.10
  303.3 2.0 fusion.2
  305.3 2.9 fusion.1
  308.2 2.0 fusion
  310.2 0.7 fusion.22
  311.0 6.4 %all-reduce = (f32[8,1,16]{2,0,1:T(8,128)}, f32[32]{0:T(128)S(1)}) all-reduce(f32[8,1,16]{2,0,1:T(8,128)S(1)} %all_to_all.22, f32[32]{0:T(128)S(1)} %reshape.191), channel_id=1, replica_groups=mesh['grp'=4,'ep'=8] {'grp'}, use_global_device_ids=true, to_apply=%region_22.23 | all-reduce | flops 160 | bytes 1280 | tf_op jit(solution)/shard_map/psum | solution.py:163
  317.4 5.8 %all-to-all-start.3 = ((f32[8,1,16]{2,1,0:T(1,128)}), f32[8,1,16]{2,1,0:T(1,128)S(1)}, u32[]{:S(2)}, u32[]{:S(2)}) async-start(f32[8,1,16]{2,1,0:T(1,128)} %bitcast.19), calls=%async_computation.6 | async-start | bytes 8192 | tf_op jit(solution)/shard_map/all_to_all | solution.py:164
  323.5 6.4 %all-to-all-done.3 = f32[8,1,16]{2,1,0:T(1,128)S(1)} async-done(((f32[8,1,16]{2,1,0:T(1,128)}), f32[8,1,16]{2,1,0:T(1,128)S(1)}, u32[]{:S(2)}, u32[]{:S(2)}) %all-to-all-start.3) | async-done | bytes 544 | tf_op jit(solution)/shard_map/all_to_all | solution.py:164
  332.4 57.6 %reduce-scatter.6.cloned.1.call-done = bf16[2,1280,96]{1,2,0:T(8,128)(2,1)} async-done(((bf16[2,1280,768]{1,2,0:T(8,128)(2,1)}), bf16[2,1280,96]{1,2,0:T(8,128)(2,1)}) %reduce-scatter.6.cloned.1.call-update) | async-done | bytes 491536 | tf_op jit(solution)/shard_map/reduce_scatter | solution.py:155
  390.0 2.0 convert_element_type.245
  392.0 85.7 %reduce-scatter.8.cloned.1.call-done = bf16[2,1280,96]{1,2,0:T(8,128)(2,1)} async-done(((bf16[2,1280,768]{1,2,0:T(8,128)(2,1)}), bf16[2,1280,96]{1,2,0:T(8,128)(2,1)}) %reduce-scatter.8.cloned.1.call-update) | async-done | bytes 491536 | tf_op jit(solution)/shard_map/reduce_scatter | solution.py:158
  477.7 2.0 convert_bitcast_fusion
  479.7 86.1 %reduce-scatter.4.cloned.1.call-done = bf16[2,1280,96]{1,2,0:T(8,128)(2,1)} async-done(((bf16[2,1280,768]{1,2,0:T(8,128)(2,1)}), bf16[2,1280,96]{1,2,0:T(8,128)(2,1)}) %reduce-scatter.4.cloned.1.call-update) | async-done | bytes 491536 | tf_op jit(solution)/shard_map/reduce_scatter | solution.py:152
  565.9 2.0 convert_element_type.242
  (75 shorter events, 8.6 us)
Async XLA Ops:
  7.2 227.2 %copy-start = (bf16[1,768,1280]{2,1,0:T(8,128)(2,1)S(1)}, bf16[1,768,1280]{2,1,0:T(8,128)(2,1)}, u32[]{:S(2)}) copy-start(bf16[1,768,1280]{2,1,0:T(8,128)(2,1)} %param.18) | copy-start | bytes 5898244
  7.2 24.8 %copy-start.2 = (bf16[256,1280]{1,0:T(8,128)(2,1)S(1)}, bf16[256,1280]{1,0:T(8,128)(2,1)}, u32[]{:S(2)}) copy-start(bf16[256,1280]{1,0:T(8,128)(2,1)} %param.11) | copy-start | bytes 1966084
  7.2 26.1 %copy-start.3 = (bf16[256,1280]{1,0:T(8,128)(2,1)S(1)}, bf16[256,1280]{1,0:T(8,128)(2,1)}, u32[]{:S(2)}) copy-start(bf16[256,1280]{1,0:T(8,128)(2,1)} %param.12) | copy-start | bytes 1966084
  7.2 81.2 %all-gather.8.cloned.1.call-start = ((), (), s32[]{:S(2)}) async-start(), calls=%async_computation.9 | async-start | bytes 4423680 | tf_op jit(solution)/shard_map/all_gather | solution.py:118
  7.9 151.8 %all-gather.6.cloned.1.call-start = ((), (), s32[]{:S(2)}) async-start(), calls=%async_computation.8 | async-start | bytes 4423680 | tf_op jit(solution)/shard_map/all_gather | solution.py:119
  8.7 221.7 %all-gather.4.cloned.1.call-start = ((), (), s32[]{:S(2)}) async-start(), calls=%async_computation.7 | async-start | bytes 4423680 | tf_op jit(solution)/shard_map/all_gather | solution.py:121
  17.9 15.6 %all-to-all-start.1 = ((bf16[8,1,16]{2,1,0:T(2,128)(2,1)}), bf16[8,1,16]{2,1,0:T(2,128)(2,1)S(1)}, u32[]{:S(2)}, u32[]{:S(2)}) async-start(bf16[8,1,16]{2,1,0:T(2,128)(2,1)} %all_to_all.24), calls=%async_computation.1 | async-start | bytes 8192 | tf_op jit(solution)/shard_map/all_to_all | solution.py:81
  33.5 18.3 %all-to-all-start = ((bf16[8,16,1280]{2,1,0:T(8,128)(2,1)}), bf16[8,16,1280]{2,1,0:T(8,128)(2,1)S(1)}, u32[]{:S(2)}, u32[]{:S(2)}) async-start(bf16[8,16,1280]{2,1,0:T(8,128)(2,1)} %bitcast.121), calls=%async_computation | async-start | bytes 655360 | tf_op jit(solution)/shard_map/all_to_all | solution.py:79
  51.8 23.6 %all-to-all-start.2 = ((bf16[8,16,1280]{2,1,0:T(8,128)(2,1)}), bf16[8,16,1280]{2,1,0:T(8,128)(2,1)S(1)}, u32[]{:S(2)}, u32[]{:S(2)}) async-start(bf16[8,16,1280]{2,1,0:T(8,128)(2,1)} %bitcast.122), calls=%async_computation.2 | async-start | bytes 655360 | tf_op jit(solution)/shard_map/all_to_all | solution.py:80
  56.7 207.0 %all-reduce.6.cloned.1.call-start = ((), (), s32[]{:S(2)}) async-start(), calls=%async_computation.13 | async-start | bytes 294912 | tf_op jit(solution)/shard_map/psum | solution.py:134
  234.3 67.2 %all-reduce.8.cloned.1.call-start = ((), (), s32[]{:S(2)}) async-start(), calls=%async_computation.14 | async-start | bytes 1179648 | tf_op jit(solution)/shard_map/psum | solution.py:98
  235.9 154.1 %reduce-scatter.6.cloned.1.call-start = ((), (), s32[]{:S(2)}) async-start(), calls=%async_computation.11 | async-start | bytes 4423680 | tf_op jit(solution)/shard_map/reduce_scatter | solution.py:155
  263.7 4.1 copy-start.5
  263.7 4.1 copy-start.6
  267.8 209.9 %reduce-scatter.8.cloned.1.call-start = ((), (), s32[]{:S(2)}) async-start(), calls=%async_computation.12 | async-start | bytes 4423680 | tf_op jit(solution)/shard_map/reduce_scatter | solution.py:158
  267.9 3.5 copy-start.9
  271.1 294.7 %reduce-scatter.4.cloned.1.call-start = ((), (), s32[]{:S(2)}) async-start(), calls=%async_computation.10 | async-start | bytes 4423680 | tf_op jit(solution)/shard_map/reduce_scatter | solution.py:152
  301.5 1.7 copy-start.4
  301.5 1.7 copy-start.7
  303.2 5.0 copy-start.8
  303.3 7.0 %copy-start.1 = (bf16[2,768,1280]{2,1,0:T(8,128)(2,1)S(1)}, bf16[2,768,1280]{2,1,0:T(8,128)(2,1)}, u32[]{:S(2)}) copy-start(bf16[2,768,1280]{2,1,0:T(8,128)(2,1)} %all-gather.4.cloned.1.call-done) | copy-start | bytes 11796484
  317.4 12.4 %all-to-all-start.3 = ((f32[8,1,16]{2,1,0:T(1,128)}), f32[8,1,16]{2,1,0:T(1,128)S(1)}, u32[]{:S(2)}, u32[]{:S(2)}) async-start(f32[8,1,16]{2,1,0:T(1,128)} %bitcast.19), calls=%async_computation.6 | async-start | bytes 8192 | tf_op jit(solution)/shard_map/all_to_all | solution.py:164
Sparse Core Ops, SparseCore 0:
  10.2 78.1 all-gather.7
  90.6 69.1 all-gather.5
  161.9 68.4 all-gather.3
  234.4 29.2 all-reduce.5
  266.9 34.6 all-reduce.7
  305.5 84.4 reduce-scatter.5
  393.7 83.9 reduce-scatter.7
  481.8 83.9 reduce-scatter.3
where the time goes:
time: 576 us; the launch traced here: 575 us
  waiting for transfers between devices  464 us (81%)
  matrix products  41.6 us (7%)
  starting transfers between devices  24.6 us (4%)
  between operations  14.4 us (2%)
  other arithmetic  12.2 us (2%)
  local copies, waits for them, and re-layouts  11.6 us (2%)
  blocking collectives  6.41 us (1%)
    reduce_scatter x1, waiting for transfers between devices, body(): lax.psum_scatter(shadow_gate.astype(jnp.bfloat16), 'ep', scatter_dimensio...  86.1 us
    reduce_scatter x1, waiting for transfers between devices, body(): lax.psum_scatter(shadow_down.astype(jnp.bfloat16), 'ep', scatter_dimensio...  85.7 us
    all_gather x1, waiting for transfers between devices, body(): lax.all_gather(up_hot, 'ep', axis=2, tiled=True)  67.5 us
    all_gather x1, waiting for transfers between devices, body(): full_down = lax.all_gather(down_hot, 'ep', axis=1, tiled=True)  66.8 us
    reduce_scatter x1, waiting for transfers between devices, body(): lax.psum_scatter(shadow_up.astype(jnp.bfloat16), 'ep', scatter_dimension=...  57.6 us
    psum x1, waiting for transfers between devices, body(): lax.psum(part_up_hot.astype(jnp.bfloat16), 'grp').astype(jnp.float32)  27.8 us
    psum x1, waiting for transfers between devices, body(): lax.psum(part_up.astype(jnp.bfloat16), 'grp').astype(jnp.float32)  26.7 us
    all_to_all x1, waiting for transfers between devices, body(): lax.all_to_all(outgoing[1], 'ep', split_axis=0, concat_axis=0, tiled=True)  13.3 us
  transfers between devices with their start and end apart: 12, of which 11 were waited for; matrix products, arithmetic and copies ran while one was open for 10% of the time, Pallas kernels for 0%

commit v1 on v0

--- a/solution.py
+++ b/solution.py
@@ -2,6 +2,28 @@
 import jax.numpy as jnp
 from jax import lax
 from jax.sharding import PartitionSpec as P
+
+
+def in_order(blocks, dim):
+    lengths = list(blocks.shape[1:])
+    lengths[dim] *= blocks.shape[0]
+    return jnp.moveaxis(blocks, 0, dim).reshape(lengths)
+
+
+def gather_around(x, axis, dim):
+    size = lax.axis_size(axis)
+    pairs = [(i, (i + 1) % size) for i in range(size)]
+    back = [(b, a) for a, b in pairs]
+    lower, upper = ([], [])
+    for hop in range(size - 1):
+        if hop % 2 == 0:
+            lower.append(lax.ppermute(lower[-1] if lower else x, axis, pairs))
+        else:
+            upper.append(lax.ppermute(upper[-1] if upper else x, axis, back))
+    blocks = jnp.stack([*lower[::-1], x, *upper])
+    shift = lax.axis_index(axis) - len(lower)
+    blocks = blocks[(jnp.arange(size) - shift) % size]
+    return in_order(blocks, dim)
 
 
 def route_table(flat_ids, targets, capacity):
@@ -118,7 +140,7 @@
         lax.all_gather(gate_hot, "ep", axis=2, tiled=True),
         lax.all_gather(up_hot, "ep", axis=2, tiled=True),
     )
-    full_down = lax.all_gather(down_hot, "ep", axis=1, tiled=True)
+    full_down = gather_around(down_hot, "ep", 1)
     hot_weighted = (
         hot_scale.astype(jnp.float32)[:, :, None] * hot_cotan.astype(jnp.float32)
     ).astype(jnp.bfloat16)

time: 576 us -> 557 us (0.967)
  waiting for transfers between devices: 464 us -> 403 us
  starting transfers between devices: 24.6 us -> 48.3 us
  local copies, waits for them, and re-layouts: 11.6 us -> 29.1 us
    all_gather x1 -> x0, waiting for transfers between devices: 66.8 us -> none  [body(): full_down = lax.all_gather(down_hot, 'ep', axis=1, tiled=True)]
    ppermute x0 -> x7, waiting for transfers between devices: none -> 50.9 us  [the longest x4 50.9 us: gather_around(): lower.append(lax.ppermute(lower[-1] if lower else x, axis, pairs))]
    ppermute x0 -> x7, starting transfers between devices: none -> 26.5 us  [the longest x3 18.6 us: gather_around(): upper.append(lax.ppermute(upper[-1] if upper else x, axis, back))]
    unnamed x23 -> x46, local copies, waits for them, and re-layouts: 3.04 us -> 17.5 us
    all_gather x1, waiting for transfers between devices: 12.9 us -> 0.01 us  [body(): lax.all_gather(gate_hot, 'ep', axis=2, tiled=True)]
    all_to_all x1, waiting for transfers between devices: 13.3 us -> 0.49 us  [body(): lax.all_to_all(outgoing[1], 'ep', split_axis=0, concat_axis=0, tiled=True)]
    all_gather x1, waiting for transfers between devices: 67.5 us -> 57.9 us  [body(): lax.all_gather(up_hot, 'ep', axis=2, tiled=True)]
    all_to_all x1, waiting for transfers between devices: 11 us -> 1.64 us  [body(): lax.all_to_all(outgoing[0], 'ep', split_axis=0, concat_axis=0, tiled=True)]
  transfers between devices with their start and end apart: 12 -> 18, of which waited for: 11 -> 13; matrix products, arithmetic and copies ran while one was open for 10% -> 13% of each run, Pallas kernels for 0% -> 0%
where the time goes in v1:
time: 557 us; the launch traced here: 555 us
  waiting for transfers between devices  403 us (72%)
  starting transfers between devices  48.3 us (9%)
  matrix products  41.6 us (7%)
  local copies, waits for them, and re-layouts  29.1 us (5%)
  between operations  14.5 us (3%)
  other arithmetic  12.2 us (2%)
  blocking collectives  6.41 us (1%)
    reduce_scatter x1, waiting for transfers between devices, body(): lax.psum_scatter(shadow_gate.astype(jnp.bfloat16), 'ep', scatter_dimensio...  86.1 us
    reduce_scatter x1, waiting for transfers between devices, body(): lax.psum_scatter(shadow_down.astype(jnp.bfloat16), 'ep', scatter_dimensio...  85.5 us
    reduce_scatter x1, waiting for transfers between devices, body(): lax.psum_scatter(shadow_up.astype(jnp.bfloat16), 'ep', scatter_dimension=...  58.2 us
    all_gather x1, waiting for transfers between devices, body(): lax.all_gather(up_hot, 'ep', axis=2, tiled=True)  57.9 us
    ppermute x4, waiting for transfers between devices, gather_around(): lower.append(lax.ppermute(lower[-1] if lower else x, axis, pairs))  50.9 us
    psum x1, waiting for transfers between devices, body(): lax.psum(part_up_hot.astype(jnp.bfloat16), 'grp').astype(jnp.float32)  27.8 us
    psum x1, waiting for transfers between devices, body(): lax.psum(part_up.astype(jnp.bfloat16), 'grp').astype(jnp.float32)  26.9 us
    ppermute x3, starting transfers between devices, gather_around(): upper.append(lax.ppermute(upper[-1] if upper else x, axis, back))  18.6 us
  transfers between devices with their start and end apart: 18, of which 13 were waited for; matrix products, arithmetic and copies ran while one was open for 13% of the time, Pallas kernels for 0%

profile of v1, /device:TPU:0, one launch (start us, length us, event | category | flops | bytes accessed | tf_op | source)
XLA Modules:
  0.0 555.4 jit_solution(9865971593276026440)
XLA Ops:
  7.9 3.0 collective-permute-start
  10.9 3.1 collective-permute-start.4
  16.2 2.3 reduce-window.14
  20.1 3.3 all-to-all-start.1
  30.5 7.1 %collective-permute-done = bf16[2,96,1280]{2,1,0:T(8,128)(2,1)} collective-permute-done((bf16[2,96,1280]{2,1,0:T(8,128)(2,1)}, bf16[2,96,1280]{2,1,0:T(8,128)(2,1)}, u32[]{:S(2)}, u32[]{:S(2)}) %collective-permute-start) | collective-permute-done | bytes 491552 | tf_op jit(solution)/shard_map/ppermute | solution.py:20
  37.6 2.5 collective-permute-start.1
  40.3 4.9 all-to-all-start
  45.2 2.1 convolution_convert_fusion.6
  47.3 12.7 %collective-permute-done.1 = bf16[2,96,1280]{2,1,0:T(8,128)(2,1)} collective-permute-done((bf16[2,96,1280]{2,1,0:T(8,128)(2,1)}, bf16[2,96,1280]{2,1,0:T(8,128)(2,1)}, u32[]{:S(2)}, u32[]{:S(2)}) %collective-permute-start.1) | collective-permute-done | bytes 491552 | tf_op jit(solution)/shard_map/ppermute | solution.py:20
  60.0 4.7 collective-permute-start.5
  66.3 7.2 %all-to-all-start.2 = ((bf16[8,16,1280]{2,1,0:T(8,128)(2,1)}), bf16[8,16,1280]{2,1,0:T(8,128)(2,1)S(1)}, u32[]{:S(2)}, u32[]{:S(2)}) async-start(bf16[8,16,1280]{2,1,0:T(8,128)(2,1)} %bitcast.5), calls=%async_computation.2 | async-start | bytes 655360 | tf_op jit(solution)/shard_map/all_to_all | solution.py:102
  73.6 2.7 fusion.16
  76.3 18.6 %collective-permute-done.2 = bf16[2,96,1280]{2,1,0:T(8,128)(2,1)} collective-permute-done((bf16[2,96,1280]{2,1,0:T(8,128)(2,1)}, bf16[2,96,1280]{2,1,0:T(8,128)(2,1)}, u32[]{:S(2)}, u32[]{:S(2)}) %collective-permute-start.2) | collective-permute-done | bytes 491552 | tf_op jit(solution)/shard_map/ppermute | solution.py:20
  94.9 2.5 collective-permute-start.3
  97.4 2.7 fusion.19
  100.7 10.7 %collective-permute-start.6 = (bf16[2,96,1280]{2,1,0:T(8,128)(2,1)}, bf16[2,96,1280]{2,1,0:T(8,128)(2,1)S(1)}, u32[]{:S(2)}, u32[]{:S(2)}) collective-permute-start(bf16[2,96,1280]{2,1,0:T(8,128)(2,1)} %collective-permute-done.5), channel_id=1, source_target_pairs={{1,0},{2,1},{3,2},{4,3},{5,4},{6,5},{7,6},{0,7},{9,8},{10,9},{11,1... | collective-permute-start | bytes 1474568 | tf_op jit(solution)/shard_map/ppermute | solution.py:22
  111.4 12.5 %collective-permute-done.3 = bf16[2,96,1280]{2,1,0:T(8,128)(2,1)} collective-permute-done((bf16[2,96,1280]{2,1,0:T(8,128)(2,1)}, bf16[2,96,1280]{2,1,0:T(8,128)(2,1)}, u32[]{:S(2)}, u32[]{:S(2)}) %collective-permute-start.3) | collective-permute-done | bytes 491552 | tf_op jit(solution)/shard_map/ppermute | solution.py:20
  123.9 1.9 bitcast_dynamic-update-slice_fusion.7
  125.8 1.9 bitcast_dynamic-update-slice_fusion.6
  127.7 1.9 bitcast_dynamic-update-slice_fusion.5
  129.6 1.8 bitcast_dynamic-update-slice_fusion.4
  131.4 1.8 bitcast_dynamic-update-slice_fusion.3
  133.3 1.9 bitcast_dynamic-update-slice_fusion.2
  135.2 1.9 bitcast_dynamic-update-slice_fusion.1
  137.8 4.9 gather_fusion
  142.7 2.4 copy.44
  145.1 2.0 copy-done.1
  147.0 1.8 convolution_convert_fusion.12
  148.8 4.0 convolution_convert_fusion.10
  152.8 57.9 %all-gather.3.cloned.1.call-done = bf16[2,1280,768]{1,2,0:T(8,128)(2,1)} async-done(((bf16[2,1280,96]{1,2,0:T(8,128)(2,1)}), bf16[2,1280,768]{1,2,0:T(8,128)(2,1)}) %all-gather.3.cloned.1.call-update) | async-done | bytes 3932176 | tf_op jit(solution)/shard_map/all_gather | solution.py:141
  210.7 3.9 convolution_convert_fusion.11
  216.1 27.8 %all-reduce.6.cloned.1.call-done = (bf16[2,16,768]{2,1,0:T(8,128)(2,1)}, bf16[2,16,768]{2,1,0:T(8,128)(2,1)}, bf16[2,16,768]{2,1,0:T(8,128)(2,1)}) async-done(((bf16[2,16,768]{2,1,0:T(8,128)(2,1)}, bf16[2,16,768]{2,1,0:T(8,128)(2,1)}, bf16[2,16,768]{2,1,0:T(8,128)(2,1)}), (bf16[2,16,768]{2,1,0:T(8,128)(2,1)}, bf16[2,16,768]{2,1,0:T(8,128)(2,1)}, bf16[2,16,768]{2,1,0:T(8,128)(2,1)})) %all-reduce.6.cloned.1.call-update) | async-done | bytes 147472 | tf_op jit(solution)/shard_map/psum | solution.py:156
  244.0 4.0 convolution_convert_fusion.1
  248.1 3.1 convolution_convert_fusion
  251.5 3.2 convolution_convert_fusion.2
  254.9 26.9 %all-reduce.8.cloned.1.call-done = (bf16[128,768]{1,0:T(8,128)(2,1)}, bf16[128,768]{1,0:T(8,128)(2,1)}, bf16[128,768]{1,0:T(8,128)(2,1)}) async-done(((bf16[128,768]{1,0:T(8,128)(2,1)}, bf16[128,768]{1,0:T(8,128)(2,1)}, bf16[128,768]{1,0:T(8,128)(2,1)}), (bf16[128,768]{1,0:T(8,128)(2,1)}, bf16[128,768]{1,0:T(8,128)(2,1)}, bf16[128,768]{1,0:T(8,128)(2,1)})) %all-reduce.8.cloned.1.call-update) | async-done | bytes 589840 | tf_op jit(solution)/shard_map/psum | solution.py:120
  283.5 2.0 fusion.2
  285.5 2.9 fusion.1
  288.5 2.0 fusion
  291.3 6.4 %all-reduce = (f32[8,1,16]{2,0,1:T(8,128)}, f32[32]{0:T(128)S(1)}) all-reduce(f32[8,1,16]{2,0,1:T(8,128)S(1)} %all_to_all.22, f32[32]{0:T(128)S(1)} %reshape.244), channel_id=1, replica_groups=mesh['grp'=4,'ep'=8] {'grp'}, use_global_device_ids=true, to_apply=%region_22.23 | all-reduce | flops 160 | bytes 1280 | tf_op jit(solution)/shard_map/psum | solution.py:185
  297.7 5.8 %all-to-all-start.3 = ((f32[8,1,16]{2,1,0:T(1,128)}), f32[8,1,16]{2,1,0:T(1,128)S(1)}, u32[]{:S(2)}, u32[]{:S(2)}) async-start(f32[8,1,16]{2,1,0:T(1,128)} %bitcast.30), calls=%async_computation.6 | async-start | bytes 8192 | tf_op jit(solution)/shard_map/all_to_all | solution.py:186
  303.8 6.4 %all-to-all-done.3 = f32[8,1,16]{2,1,0:T(1,128)S(1)} async-done(((f32[8,1,16]{2,1,0:T(1,128)}), f32[8,1,16]{2,1,0:T(1,128)S(1)}, u32[]{:S(2)}, u32[]{:S(2)}) %all-to-all-start.3) | async-done | bytes 544 | tf_op jit(solution)/shard_map/all_to_all | solution.py:186
  312.6 58.2 %reduce-scatter.6.cloned.1.call-done = bf16[2,1280,96]{1,2,0:T(8,128)(2,1)} async-done(((bf16[2,1280,768]{1,2,0:T(8,128)(2,1)}), bf16[2,1280,96]{1,2,0:T(8,128)(2,1)}) %reduce-scatter.6.cloned.1.call-update) | async-done | bytes 491536 | tf_op jit(solution)/shard_map/reduce_scatter | solution.py:177
  370.8 2.0 convert_element_type.245
  372.9 85.5 %reduce-scatter.8.cloned.1.call-done = bf16[2,1280,96]{1,2,0:T(8,128)(2,1)} async-done(((bf16[2,1280,768]{1,2,0:T(8,128)(2,1)}), bf16[2,1280,96]{1,2,0:T(8,128)(2,1)}) %reduce-scatter.8.cloned.1.call-update) | async-done | bytes 491536 | tf_op jit(solution)/shard_map/reduce_scatter | solution.py:180
  458.4 2.0 convert_bitcast_fusion
  460.4 86.1 %reduce-scatter.4.cloned.1.call-done = bf16[2,1280,96]{1,2,0:T(8,128)(2,1)} async-done(((bf16[2,1280,768]{1,2,0:T(8,128)(2,1)}), bf16[2,1280,96]{1,2,0:T(8,128)(2,1)}) %reduce-scatter.4.cloned.1.call-update) | async-done | bytes 491536 | tf_op jit(solution)/shard_map/reduce_scatter | solution.py:174
  546.5 2.0 convert_element_type.242
  (114 shorter events, 22.0 us)
Async XLA Ops:
  7.2 207.4 %copy-start = (bf16[1,768,1280]{2,1,0:T(8,128)(2,1)S(1)}, bf16[1,768,1280]{2,1,0:T(8,128)(2,1)}, u32[]{:S(2)}) copy-start(bf16[1,768,1280]{2,1,0:T(8,128)(2,1)} %param.18) | copy-start | bytes 5898244
  7.2 21.4 %copy-start.3 = (bf16[256,1280]{1,0:T(8,128)(2,1)S(1)}, bf16[256,1280]{1,0:T(8,128)(2,1)}, u32[]{:S(2)}) copy-start(bf16[256,1280]{1,0:T(8,128)(2,1)} %param.11) | copy-start | bytes 1966084
  7.2 141.6 %all-gather.5.cloned.1.call-start = ((), (), s32[]{:S(2)}) async-start(), calls=%async_computation.8 | async-start | bytes 4423680 | tf_op jit(solution)/shard_map/all_gather | solution.py:140
  7.9 29.7 %collective-permute-start = (bf16[2,96,1280]{2,1,0:T(8,128)(2,1)}, bf16[2,96,1280]{2,1,0:T(8,128)(2,1)}, u32[]{:S(2)}, u32[]{:S(2)}) collective-permute-start(bf16[2,96,1280]{2,1,0:T(8,128)(2,1)} %param.21), channel_id=1, source_target_pairs={{0,1},{1,2},{2,3},{3,4},{4,5},{5,6},{6,7},{7,0},{8,9},{9,10},{10,1... | collective-permute-start | bytes 1474568 | tf_op jit(solution)/shard_map/ppermute | solution.py:20
  10.9 49.0 %collective-permute-start.4 = (bf16[2,96,1280]{2,1,0:T(8,128)(2,1)}, bf16[2,96,1280]{2,1,0:T(8,128)(2,1)}, u32[]{:S(2)}, u32[]{:S(2)}) collective-permute-start(bf16[2,96,1280]{2,1,0:T(8,128)(2,1)} %param.21), channel_id=1, source_target_pairs={{1,0},{2,1},{3,2},{4,3},{5,4},{6,5},{7,6},{0,7},{9,8},{10,9},{11,1... | collective-permute-start | bytes 1474568 | tf_op jit(solution)/shard_map/ppermute | solution.py:22
  19.1 10.2 %copy-start.14 = (pred[1536]{0:T(1024)(128)(4,1)}, pred[1536]{0:T(1024)(128)(4,1)S(1)}, u32[]{:S(2)}) copy-start(pred[1536]{0:T(1024)(128)(4,1)S(1)} %broadcast_compare_fusion.1) | copy-start | bytes 4612
  19.1 9.7 %copy-start.10 = (s32[1536]{0:T(1024)}, s32[1536]{0:T(1024)S(1)}, u32[]{:S(2)}) copy-start(s32[1536]{0:T(1024)S(1)} %multiply_add_fusion.1) | copy-start | bytes 18436
  20.1 20.2 %all-to-all-start.1 = ((bf16[8,1,16]{2,1,0:T(2,128)(2,1)}), bf16[8,1,16]{2,1,0:T(2,128)(2,1)S(1)}, u32[]{:S(2)}, u32[]{:S(2)}) async-start(bf16[8,1,16]{2,1,0:T(2,128)(2,1)} %all_to_all.24), calls=%async_computation.1 | async-start | bytes 8192 | tf_op jit(solution)/shard_map/all_to_all | solution.py:103
  23.4 187.3 %all-gather.3.cloned.1.call-start = ((), (), s32[]{:S(2)}) async-start(), calls=%async_computation.7 | async-start | bytes 4423680 | tf_op jit(solution)/shard_map/all_gather | solution.py:141
  26.7 13.6 %copy-start.12 = (s32[1536]{0:T(1024)}, s32[1536]{0:T(1024)S(1)}, u32[]{:S(2)}) copy-start(s32[1536]{0:T(1024)S(1)} %multiply_add_fusion) | copy-start | bytes 18436
  26.9 13.3 %copy-start.16 = (pred[1536]{0:T(1024)(128)(4,1)}, pred[1536]{0:T(1024)(128)(4,1)S(1)}, u32[]{:S(2)}) copy-start(pred[1536]{0:T(1024)(128)(4,1)S(1)} %broadcast_compare_fusion) | copy-start | bytes 4612
  37.6 22.4 %collective-permute-start.1 = (bf16[2,96,1280]{2,1,0:T(8,128)(2,1)}, bf16[2,96,1280]{2,1,0:T(8,128)(2,1)}, u32[]{:S(2)}, u32[]{:S(2)}) collective-permute-start(bf16[2,96,1280]{2,1,0:T(8,128)(2,1)} %collective-permute-done), channel_id=1, source_target_pairs={{0,1},{1,2},{2,3},{3,4},{4,5},{5,6},{6,7},{7,0},{8,9},{9,10},{10,1... | collective-permute-start | bytes 1474568 | tf_op jit(solution)/shard_map/ppermute | solution.py:20
  40.3 26.1 %all-to-all-start = ((bf16[8,16,1280]{2,1,0:T(8,128)(2,1)}), bf16[8,16,1280]{2,1,0:T(8,128)(2,1)S(1)}, u32[]{:S(2)}, u32[]{:S(2)}) async-start(bf16[8,16,1280]{2,1,0:T(8,128)(2,1)} %bitcast.1), calls=%async_computation | async-start | bytes 655360 | tf_op jit(solution)/shard_map/all_to_all | solution.py:101
  60.0 35.0 %collective-permute-start.2 = (bf16[2,96,1280]{2,1,0:T(8,128)(2,1)}, bf16[2,96,1280]{2,1,0:T(8,128)(2,1)}, u32[]{:S(2)}, u32[]{:S(2)}) collective-permute-start(bf16[2,96,1280]{2,1,0:T(8,128)(2,1)} %collective-permute-done.1), channel_id=1, source_target_pairs={{0,1},{1,2},{2,3},{3,4},{4,5},{5,6},{6,7},{7,0},{8,9},{9,10},{10,1... | collective-permute-start | bytes 1474568 | tf_op jit(solution)/shard_map/ppermute | solution.py:20
  60.0 40.7 %collective-permute-start.5 = (bf16[2,96,1280]{2,1,0:T(8,128)(2,1)}, bf16[2,96,1280]{2,1,0:T(8,128)(2,1)}, u32[]{:S(2)}, u32[]{:S(2)}) collective-permute-start(bf16[2,96,1280]{2,1,0:T(8,128)(2,1)} %collective-permute-done.4), channel_id=1, source_target_pairs={{1,0},{2,1},{3,2},{4,3},{5,4},{6,5},{7,6},{0,7},{9,8},{10,9},{11,1... | collective-permute-start | bytes 1474568 | tf_op jit(solution)/shard_map/ppermute | solution.py:22
  66.3 34.2 %all-to-all-start.2 = ((bf16[8,16,1280]{2,1,0:T(8,128)(2,1)}), bf16[8,16,1280]{2,1,0:T(8,128)(2,1)S(1)}, u32[]{:S(2)}, u32[]{:S(2)}) async-start(bf16[8,16,1280]{2,1,0:T(8,128)(2,1)} %bitcast.5), calls=%async_computation.2 | async-start | bytes 655360 | tf_op jit(solution)/shard_map/all_to_all | solution.py:102
  73.6 170.4 %all-reduce.6.cloned.1.call-start = ((), (), s32[]{:S(2)}) async-start(), calls=%async_computation.12 | async-start | bytes 294912 | tf_op jit(solution)/shard_map/psum | solution.py:156
  94.9 29.0 %collective-permute-start.3 = (bf16[2,96,1280]{2,1,0:T(8,128)(2,1)}, bf16[2,96,1280]{2,1,0:T(8,128)(2,1)}, u32[]{:S(2)}, u32[]{:S(2)}) collective-permute-start(bf16[2,96,1280]{2,1,0:T(8,128)(2,1)} %collective-permute-done.2), channel_id=1, source_target_pairs={{0,1},{1,2},{2,3},{3,4},{4,5},{5,6},{6,7},{7,0},{8,9},{9,10},{10,1... | collective-permute-start | bytes 1474568 | tf_op jit(solution)/shard_map/ppermute | solution.py:20
  100.7 36.3 %collective-permute-start.6 = (bf16[2,96,1280]{2,1,0:T(8,128)(2,1)}, bf16[2,96,1280]{2,1,0:T(8,128)(2,1)S(1)}, u32[]{:S(2)}, u32[]{:S(2)}) collective-permute-start(bf16[2,96,1280]{2,1,0:T(8,128)(2,1)} %collective-permute-done.5), channel_id=1, source_target_pairs={{1,0},{2,1},{3,2},{4,3},{5,4},{6,5},{7,6},{0,7},{9,8},{10,9},{11,1... | collective-permute-start | bytes 1474568 | tf_op jit(solution)/shard_map/ppermute | solution.py:22
  145.1 2.0 copy-start.1
  214.5 67.3 %all-reduce.8.cloned.1.call-start = ((), (), s32[]{:S(2)}) async-start(), calls=%async_computation.13 | async-start | bytes 1179648 | tf_op jit(solution)/shard_map/psum | solution.py:120
  216.1 154.7 %reduce-scatter.6.cloned.1.call-start = ((), (), s32[]{:S(2)}) async-start(), calls=%async_computation.10 | async-start | bytes 4423680 | tf_op jit(solution)/shard_map/reduce_scatter | solution.py:177
  244.0 4.1 copy-start.5
  244.0 4.1 copy-start.6
  248.0 210.4 %reduce-scatter.8.cloned.1.call-start = ((), (), s32[]{:S(2)}) async-start(), calls=%async_computation.11 | async-start | bytes 4423680 | tf_op jit(solution)/shard_map/reduce_scatter | solution.py:180
  248.1 3.4 copy-start.9
  251.2 295.3 %reduce-scatter.4.cloned.1.call-start = ((), (), s32[]{:S(2)}) async-start(), calls=%async_computation.9 | async-start | bytes 4423680 | tf_op jit(solution)/shard_map/reduce_scatter | solution.py:174
  281.8 1.7 copy-start.4
  281.8 1.7 copy-start.7
  283.4 5.0 copy-start.8
  283.5 7.0 %copy-start.2 = (bf16[2,8,96,1280]{3,2,1,0:T(8,128)(2,1)S(1)}, bf16[2,8,96,1280]{3,2,1,0:T(8,128)(2,1)}, u32[]{:S(2)}) copy-start(bf16[2,8,96,1280]{3,2,1,0:T(8,128)(2,1)} %copy-done.1) | copy-start | bytes 11796484
  288.5 15.1 %copy-start.13 = (s32[1536]{0:T(1024)S(1)}, s32[1536]{0:T(1024)}, u32[]{:S(2)}) copy-start(s32[1536]{0:T(1024)} %copy-done.12) | copy-start | bytes 18436
  288.5 15.1 %copy-start.17 = (pred[1536]{0:T(1024)(128)(4,1)S(1)}, pred[1536]{0:T(1024)(128)(4,1)}, u32[]{:S(2)}) copy-start(pred[1536]{0:T(1024)(128)(4,1)} %copy-done.16) | copy-start | bytes 4612
  288.5 22.9 %copy-start.11 = (s32[1536]{0:T(1024)S(1)}, s32[1536]{0:T(1024)}, u32[]{:S(2)}) copy-start(s32[1536]{0:T(1024)} %copy-done.10) | copy-start | bytes 18436
  288.5 22.9 %copy-start.15 = (pred[1536]{0:T(1024)(128)(4,1)S(1)}, pred[1536]{0:T(1024)(128)(4,1)}, u32[]{:S(2)}) copy-start(pred[1536]{0:T(1024)(128)(4,1)} %copy-done.14) | copy-start | bytes 4612
  297.7 12.4 %all-to-all-start.3 = ((f32[8,1,16]{2,1,0:T(1,128)}), f32[8,1,16]{2,1,0:T(1,128)S(1)}, u32[]{:S(2)}, u32[]{:S(2)}) async-start(f32[8,1,16]{2,1,0:T(1,128)} %bitcast.30), calls=%async_computation.6 | async-start | bytes 8192 | tf_op jit(solution)/shard_map/all_to_all | solution.py:186
Sparse Core Ops, SparseCore 0:
  10.2 128.9 all-gather.4
  141.4 69.2 all-gather.2
  214.7 29.2 all-reduce.5
  247.1 34.6 all-reduce.7
  285.8 84.9 reduce-scatter.5
  374.4 83.9 reduce-scatter.7
  462.5 83.9 reduce-scatter.3
